TPU v7x, 128 devices: a whole 4x4x4 slice. The times are simulated.
128 devices in a mesh: row: 4 (over z), col: 32 (over x, y, core).
Axes of the slice: x: 4, y: 4, z: 4, core: 2. Of those that a mesh axis runs over, the one named last changes fastest.
Arguments:
- matrix_real: bfloat16 [512, 16384], P('col', 'row'), may hold values from -0.25 to 0.25
- matrix_imag: bfloat16 [512, 16384], P('col', 'row'), may hold values from -0.25 to 0.25
- valence_index: int32 [512], P('col'), may hold values from 0 to 15
- conduction_index: int32 [512], P('col'), may hold values from 0 to 31
- valence_energy: float32 [16], replicated, may hold values from -1.5 to -0.1
- conduction_energy: float32 [32], replicated, may hold values from 0.1 to 2
- frequency: float32 [2], replicated, may hold values from 0.2 to 2
Outputs:
- chi_real: bfloat16 [2, 16384, 16384], P(None, 'row', 'col')
- chi_imag: bfloat16 [2, 16384, 16384], P(None, 'row', 'col')
All inputs are finite; a program needn't handle non-finite values.
Results may differ from a plain program's by a relative error of at most 0.005.
Values may be sent and summed in bfloat16 or wider, within the bound.
No kernel may reach another device: no remote copies, remote signals or barrier semaphores. Data moves between devices by JAX's collectives and lax.ppermute only.
A program may use at most 192 MiB of HBM per device.

v0:
```python
import jax
import jax.numpy as jnp
from jax import lax
from jax.sharding import PartitionSpec as P


def lookup(indices, table):
    count = table.shape[0]
    picks = indices[:, None] == lax.broadcasted_iota(jnp.int32, (1, count), 1)
    return jnp.sum(jnp.where(picks, table[None, :], 0.0), axis=1)


def contract(left_side, right_side):
    return lax.dot_general(
        left_side, right_side, (((0,), (0,)), ((), ())), preferred_element_type=jnp.float32
    )


CHUNKS = 4


def on_device(
    matrix_real,
    matrix_imag,
    valence_index,
    conduction_index,
    valence_energy,
    conduction_energy,
    frequency,
):
    ncol = lax.psum(1, "col")
    local_pairs, local_g = matrix_real.shape
    pairs = local_pairs * ncol
    both = jnp.stack([matrix_real, matrix_imag])
    bands = jnp.stack([valence_index, conduction_index]).astype(jnp.float32)
    all_bands = lax.all_gather(bands, "col", axis=1, tiled=True).astype(jnp.int32)
    gap = lookup(all_bands[1], conduction_energy) - lookup(all_bands[0], valence_energy)
    spread = lax.all_gather(both, "row", axis=2, tiled=True)
    spread = spread.reshape(2, local_pairs, ncol, -1)
    column = lax.all_to_all(spread, "col", split_axis=2, concat_axis=1, tiled=True)
    width = column.shape[-1]
    wide = column.reshape(2, pairs, width).astype(jnp.float32)
    right_real = []
    right_imag = []
    for index in range(frequency.shape[0]):
        omega = frequency[index]
        weight = 4.0 * gap / (gap * gap + omega * omega)
        scaled_real = (weight[:, None] * wide[0]).astype(jnp.bfloat16)
        scaled_imag = (weight[:, None] * wide[1]).astype(jnp.bfloat16)
        right_real.append(jnp.concatenate([-scaled_real, -scaled_imag], axis=0))
        right_imag.append(jnp.concatenate([-scaled_imag, scaled_real], axis=0))
    step = local_g // CHUNKS
    real_parts = [[] for _ in right_real]
    imag_parts = [[] for _ in right_real]
    for chunk in range(CHUNKS):
        piece = both[:, :, chunk * step : (chunk + 1) * step]
        left = lax.all_gather(piece, "col", axis=1, tiled=True).reshape(2 * pairs, step)
        for index in range(len(right_real)):
            real_parts[index].append(contract(left, right_real[index]).astype(jnp.bfloat16))
            imag_parts[index].append(contract(left, right_imag[index]).astype(jnp.bfloat16))
    chi_real = jnp.stack([jnp.concatenate(p, axis=0) for p in real_parts])
    chi_imag = jnp.stack([jnp.concatenate(p, axis=0) for p in imag_parts])
    return (chi_real, chi_imag)


def solution(mesh):
    placed = (P("col", "row"), P("col", "row"), P("col"), P("col"), P(), P(), P())
    return jax.shard_map(
        on_device,
        mesh=mesh,
        in_specs=placed,
        out_specs=(P(None, "row", "col"), P(None, "row", "col")),
        check_vma=False,
    )
```

profile of v0, /device:TPU:1, one launch (start us, length us, event | category | flops | bytes accessed | tf_op | source)
XLA Modules:
  0.0 271.8 jit_solution(17406845412309366294)
XLA Ops:
  7.2 0.0 all-gather.9.cloned.1.call-start
  7.2 1.7 pad_maximum_fusion.6
  8.9 0.0 all-gather.9.cloned.1.call-update
  8.9 0.0 all-gather.11.cloned.1.call-start
  9.0 1.6 fusion.6
  10.6 0.0 all-gather.11.cloned.1.call-update
  10.6 0.0 all-gather.7.cloned.1.call-start
  10.6 0.7 all-gather.7.cloned.1.call-update
  11.3 0.0 all-gather.13.cloned.1.call-start
  11.4 0.5 all-gather.13.cloned.1.call-update
  11.9 24.9 %all-gather.9.cloned.1.call-done = bf16[2,16,16384]{2,1,0:T(8,128)(2,1)} async-done(((bf16[2,16,4096]{2,1,0:T(8,128)(2,1)}), bf16[2,16,16384]{2,1,0:T(8,128)(2,1)}) %all-gather.9.cloned.1.call-update) | async-done | bytes 1048592 | tf_op jit(solution)/shard_map/all_gather | solution.py:38
  36.8 2.4 copy.26
  39.2 8.4 %all-to-all-start = ((bf16[2,16,32,512]{3,1,0,2:T(8,128)(2,1)}), bf16[2,16,32,512]{3,1,0,2:T(8,128)(2,1)S(1)}, u32[]{:S(2)}, u32[]{:S(2)}) async-start(bf16[2,16,32,512]{3,1,0,2:T(8,128)(2,1)} %bitcast.71), calls=%async_computation | async-start | bytes 2097152 | tf_op jit(solution)/shard_map/all_to_all | solution.py:40
  47.6 0.0 all-gather.15.cloned.1.call-start
  47.7 0.5 all-gather.15.cloned.1.call-update
  48.2 0.0 copy-done.12
  48.2 0.6 fusion.17
  51.3 0.0 copy-done.15
  51.3 0.0 copy-done.16
  51.3 29.0 %all-gather = f32[32,16,2]{1,2,0:T(2,128)S(1)} all-gather(f32[1,16,2]{1,2,0:T(2,128)S(1)} %fusion.10), channel_id=1, replica_groups=mesh['row'=4,'col'=32] {'col'}, dimensions={0}, use_global_device_ids=true | all-gather | bytes 4224 | tf_op jit(solution)/shard_map/all_gather | solution.py:36
  80.3 0.1 copy.19
  80.4 0.1 copy.20
  80.5 0.1 reshape.57
  80.6 0.1 select_reduce_fusion.1
  80.7 0.1 select_reduce_fusion
  80.8 0.0 all-to-all-done
  80.8 0.3 convert_bitcast_fusion
  81.1 0.2 fusion.15
  81.3 1.4 fusion.5
  82.7 5.7 %all-gather.11.cloned.1.call-done = bf16[2,512,1024]{2,1,0:T(8,128)(2,1)} async-done(((bf16[2,16,1024]{2,1,0:T(8,128)(2,1)}), bf16[2,512,1024]{2,1,0:T(8,128)(2,1)}) %all-gather.11.cloned.1.call-update) | async-done | bytes 2097168 | tf_op jit(solution)/shard_map/all_gather | solution.py:57
  88.4 3.8 %convolution_convert_fusion.10 = bf16[1024,512]{1,0:T(8,128)(2,1)} fusion(bf16[1024,1024]{1,0:T(8,128)(2,1)} %bitcast.82, bf16[512,512]{1,0:T(8,128)(2,1)S(1)} %get-tuple-element.11, bf16[512,512]{1,0:T(8,128)(2,1)S(1)} %get-tuple-element.16), kind=kOutput, calls=%fused_computation.17 | convolution fusion | flops 1076363264 | bytes 4194304 | tf_op jit(solution)/shard_map/dot_general | solution.py:14
  92.3 41.5 %all-gather.7.cloned.1.call-done = bf16[2,512,1024]{2,1,0:T(8,128)(2,1)} async-done(((bf16[2,16,1024]{2,1,0:T(8,128)(2,1)}), bf16[2,512,1024]{2,1,0:T(8,128)(2,1)}) %all-gather.7.cloned.1.call-update) | async-done | bytes 2097168 | tf_op jit(solution)/shard_map/all_gather | solution.py:57
  133.8 4.0 %convolution_convert_fusion.11 = bf16[1024,512]{1,0:T(8,128)(2,1)} fusion(bf16[1024,1024]{1,0:T(8,128)(2,1)} %bitcast.86, bf16[512,512]{1,0:T(8,128)(2,1)S(1)} %get-tuple-element.11, bf16[512,512]{1,0:T(8,128)(2,1)S(1)} %get-tuple-element.16), kind=kOutput, calls=%fused_computation.18 | convolution fusion | flops 1076363264 | bytes 4194304 | tf_op jit(solution)/shard_map/dot_general | solution.py:14
  137.7 0.0 copy-done.19
  137.8 0.0 copy-start.17
  137.8 1.3 convolution_convert_fusion.3
  139.1 0.3 copy-done.17
  139.3 2.5 convolution_convert_fusion.2
  141.9 37.1 %all-gather.13.cloned.1.call-done = bf16[2,512,1024]{2,1,0:T(8,128)(2,1)} async-done(((bf16[2,16,1024]{2,1,0:T(8,128)(2,1)}), bf16[2,512,1024]{2,1,0:T(8,128)(2,1)}) %all-gather.13.cloned.1.call-update) | async-done | bytes 2097168 | tf_op jit(solution)/shard_map/all_gather | solution.py:57
  179.0 4.2 %convolution_convert_fusion.9 = bf16[1024,512]{1,0:T(8,128)(2,1)} fusion(bf16[1024,1024]{1,0:T(8,128)(2,1)} %bitcast.90, bf16[512,512]{1,0:T(8,128)(2,1)} %copy-done.5, bf16[512,512]{1,0:T(8,128)(2,1)} %copy-done.11), kind=kOutput, calls=%fused_computation.16 | convolution fusion | flops 1076363264 | bytes 4194304 | tf_op jit(solution)/shard_map/dot_general | solution.py:14
  183.2 2.3 convolution_convert_fusion.1
  185.5 38.7 %all-gather.15.cloned.1.call-done = bf16[2,512,1024]{2,1,0:T(8,128)(2,1)} async-done(((bf16[2,16,1024]{2,1,0:T(8,128)(2,1)}), bf16[2,512,1024]{2,1,0:T(8,128)(2,1)}) %all-gather.15.cloned.1.call-update) | async-done | bytes 2097168 | tf_op jit(solution)/shard_map/all_gather | solution.py:57
  224.2 3.3 %convolution_convert_fusion.8 = bf16[1024,512]{1,0:T(8,128)(2,1)S(1)} fusion(bf16[1024,1024]{1,0:T(8,128)(2,1)} %bitcast.94, bf16[512,512]{1,0:T(8,128)(2,1)} %copy-done.5, bf16[512,512]{1,0:T(8,128)(2,1)} %copy-done.11), kind=kOutput, calls=%fused_computation.15 | convolution fusion | flops 1076363264 | bytes 4194304 | tf_op jit(solution)/shard_map/dot_general | solution.py:14
  227.5 0.0 copy-done.7
  227.5 0.0 copy-done.10
  227.5 0.0 copy-done.23
  227.5 0.0 copy-start.3
  227.5 0.0 copy-start.18
  227.5 2.3 convolution_convert_fusion
  229.8 1.3 convolution_convert_fusion.14
  231.1 0.3 copy-done.22
  231.4 1.3 convolution_convert_fusion.13
  232.7 2.5 convolution_convert_fusion.6
  235.2 2.3 convolution_convert_fusion.5
  237.5 1.3 convolution_convert_fusion.12
  238.8 2.4 convolution_convert_fusion.4
  241.2 2.3 convolution_convert_fusion.7
  243.4 1.3 convolution_convert_fusion.15
  244.7 0.2 copy-done.1
  245.0 0.3 copy-done.2
  245.3 2.8 %maximum_bitcast_fusion = (bf16[1,4096,512]{2,1,0:T(8,128)(2,1)S(1)}, bf16[1,4096,512]{2,1,0:T(8,128)(2,1)}) fusion(bf16[1024,512]{1,0:T(8,128)(2,1)S(1)} %convolution_convert_fusion.12, bf16[1024,512]{1,0:T(8,128)(2,1)S(1)} %convolution_convert_fusion.13, bf16[1024,512]{1,0:T(8,128)(2,1)S(1)} %convolution_convert_fusion.14, ...), kind=kLoop, calls=%fused_computation.2 | loop fusion | flops 33554432 | bytes 16777216 | tf_op jit(solution)/shard_map/stack | solution.py:61
  248.1 6.3 %pad_maximum_fusion = bf16[2,4096,512]{2,1,0:T(8,128)(2,1)} fusion(bf16[1,4096,512]{2,1,0:T(8,128)(2,1)} %get-tuple-element.27, bf16[1,4096,512]{2,1,0:T(8,128)(2,1)S(1)} %get-tuple-element.26), kind=kLoop, calls=%fused_computation | loop fusion | flops 4194304 | bytes 16777216 | tf_op jit(solution)/shard_map/stack | solution.py:61
  254.5 4.4 %maximum_bitcast_fusion.2 = (bf16[1,4096,512]{2,1,0:T(8,128)(2,1)S(1)}, bf16[1,4096,512]{2,1,0:T(8,128)(2,1)}) fusion(bf16[1024,512]{1,0:T(8,128)(2,1)} %convolution_convert_fusion.4, bf16[1024,512]{1,0:T(8,128)(2,1)} %convolution_convert_fusion.5, bf16[1024,512]{1,0:T(8,128)(2,1)} %convolution_convert_fusion.6, ...), kind=kLoop, calls=%fused_computation.4 | loop fusion | flops 33554432 | bytes 16777216 | tf_op jit(solution)/shard_map/stack | solution.py:62
  258.9 6.3 %pad_maximum_fusion.1 = bf16[2,4096,512]{2,1,0:T(8,128)(2,1)} fusion(bf16[1,4096,512]{2,1,0:T(8,128)(2,1)} %get-tuple-element.29, bf16[1,4096,512]{2,1,0:T(8,128)(2,1)S(1)} %get-tuple-element.28), kind=kLoop, calls=%fused_computation.1 | loop fusion | flops 4194304 | bytes 16777216 | tf_op jit(solution)/shard_map/stack | solution.py:62
  (38 shorter events, 0.1 us)
Async XLA Ops:
  7.2 29.6 %all-gather.9.cloned.1.call-start = ((), (), s32[]{:S(2)}) async-start(), calls=%async_computation.2 | async-start | bytes 1310720 | tf_op jit(solution)/shard_map/all_gather | solution.py:38
  8.9 79.5 %all-gather.11.cloned.1.call-start = ((), (), s32[]{:S(2)}) async-start(), calls=%async_computation.3 | async-start | bytes 2162688 | tf_op jit(solution)/shard_map/all_gather | solution.py:57
  10.6 123.2 %all-gather.7.cloned.1.call-start = ((), (), s32[]{:S(2)}) async-start(), calls=%async_computation.1 | async-start | bytes 2162688 | tf_op jit(solution)/shard_map/all_gather | solution.py:57
  11.3 167.7 %all-gather.13.cloned.1.call-start = ((), (), s32[]{:S(2)}) async-start(), calls=%async_computation.4 | async-start | bytes 2162688 | tf_op jit(solution)/shard_map/all_gather | solution.py:57
  36.8 11.5 %copy-start.12 = (f32[2]{0:T(128)S(1)}, f32[2]{0:T(128)}, u32[]{:S(2)}) copy-start(f32[2]{0:T(128)} %param.13) | copy-start | bytes 28
  36.8 14.5 %copy-start.15 = (s32[16]{0:T(128)S(1)}, s32[16]{0:T(128)}, u32[]{:S(2)}) copy-start(s32[16]{0:T(128)} %param.10) | copy-start | bytes 196
  36.8 14.5 %copy-start.16 = (s32[16]{0:T(128)S(1)}, s32[16]{0:T(128)}, u32[]{:S(2)}) copy-start(s32[16]{0:T(128)} %param.9) | copy-start | bytes 196
  36.8 43.8 %copy-start.13 = (f32[16]{0:T(128)S(1)}, f32[16]{0:T(128)}, u32[]{:S(2)}) copy-start(f32[16]{0:T(128)} %param.11) | copy-start | bytes 196
  36.8 43.9 %copy-start.14 = (f32[32]{0:T(128)S(1)}, f32[32]{0:T(128)}, u32[]{:S(2)}) copy-start(f32[32]{0:T(128)} %param.12) | copy-start | bytes 388
  39.2 41.6 %all-to-all-start = ((bf16[2,16,32,512]{3,1,0,2:T(8,128)(2,1)}), bf16[2,16,32,512]{3,1,0,2:T(8,128)(2,1)S(1)}, u32[]{:S(2)}, u32[]{:S(2)}) async-start(bf16[2,16,32,512]{3,1,0,2:T(8,128)(2,1)} %bitcast.71), calls=%async_computation | async-start | bytes 2097152 | tf_op jit(solution)/shard_map/all_to_all | solution.py:40
  47.6 176.6 %all-gather.15.cloned.1.call-start = ((), (), s32[]{:S(2)}) async-start(), calls=%async_computation.5 | async-start | bytes 2162688 | tf_op jit(solution)/shard_map/all_gather | solution.py:57
  82.7 51.0 %copy-start.11 = (bf16[512,512]{1,0:T(8,128)(2,1)}, bf16[512,512]{1,0:T(8,128)(2,1)S(1)}, u32[]{:S(2)}) copy-start(bf16[512,512]{1,0:T(8,128)(2,1)S(1)} %get-tuple-element.16) | copy-start | bytes 1572868
  82.7 55.0 %copy-start.5 = (bf16[512,512]{1,0:T(8,128)(2,1)}, bf16[512,512]{1,0:T(8,128)(2,1)S(1)}, u32[]{:S(2)}) copy-start(bf16[512,512]{1,0:T(8,128)(2,1)S(1)} %get-tuple-element.11) | copy-start | bytes 1572868
  82.7 55.0 %copy-start.8 = (bf16[512,512]{1,0:T(8,128)(2,1)}, bf16[512,512]{1,0:T(8,128)(2,1)S(1)}, u32[]{:S(2)}) copy-start(bf16[512,512]{1,0:T(8,128)(2,1)S(1)} %get-tuple-element.17) | copy-start | bytes 1572868
  133.7 4.0 %copy-start.19 = (bf16[2,512,1024]{2,1,0:T(8,128)(2,1)S(1)}, bf16[2,512,1024]{2,1,0:T(8,128)(2,1)}, u32[]{:S(2)}) copy-start(bf16[2,512,1024]{2,1,0:T(8,128)(2,1)} %all-gather.7.cloned.1.call-done) | copy-start | bytes 6291460
  137.8 1.6 copy-start.17
  179.0 4.2 %copy-start.6 = (bf16[512,512]{1,0:T(8,128)(2,1)S(1)}, bf16[512,512]{1,0:T(8,128)(2,1)}, u32[]{:S(2)}) copy-start(bf16[512,512]{1,0:T(8,128)(2,1)} %copy-done.5) | copy-start | bytes 1572868
  179.0 4.2 %copy-start.9 = (bf16[512,512]{1,0:T(8,128)(2,1)S(1)}, bf16[512,512]{1,0:T(8,128)(2,1)}, u32[]{:S(2)}) copy-start(bf16[512,512]{1,0:T(8,128)(2,1)} %copy-done.8) | copy-start | bytes 1572868
  179.0 4.2 %copy-start.21 = (bf16[2,512,1024]{2,1,0:T(8,128)(2,1)S(1)}, bf16[2,512,1024]{2,1,0:T(8,128)(2,1)}, u32[]{:S(2)}) copy-start(bf16[2,512,1024]{2,1,0:T(8,128)(2,1)} %all-gather.13.cloned.1.call-done) | copy-start | bytes 6291460
  224.2 3.3 %copy-start.7 = (bf16[512,512]{1,0:T(8,128)(2,1)S(1)}, bf16[512,512]{1,0:T(8,128)(2,1)}, u32[]{:S(2)}) copy-start(bf16[512,512]{1,0:T(8,128)(2,1)} %copy-done.5) | copy-start | bytes 1572868
  224.2 3.3 %copy-start.10 = (bf16[512,512]{1,0:T(8,128)(2,1)S(1)}, bf16[512,512]{1,0:T(8,128)(2,1)}, u32[]{:S(2)}) copy-start(bf16[512,512]{1,0:T(8,128)(2,1)} %copy-done.8) | copy-start | bytes 1572868
  224.2 3.3 %copy-start.23 = (bf16[2,512,1024]{2,1,0:T(8,128)(2,1)S(1)}, bf16[2,512,1024]{2,1,0:T(8,128)(2,1)}, u32[]{:S(2)}) copy-start(bf16[2,512,1024]{2,1,0:T(8,128)(2,1)} %all-gather.15.cloned.1.call-done) | copy-start | bytes 6291460
  227.5 2.3 copy-start.3
  227.5 2.3 copy-start.18
  229.8 1.6 copy-start.22
  231.4 1.3 copy-start.4
  238.8 2.4 copy-start.20
  243.4 1.3 copy-start
  243.4 1.5 copy-start.1
  243.4 1.9 copy-start.2
Sparse Core Ops, SparseCore 0:
  10.2 26.4 all-gather.8
  39.7 48.6 all-gather.10
  90.8 42.9 all-gather.6
  136.0 42.9 all-gather.12
  181.2 42.9 all-gather.14
where the time goes:
time: 272 us
  waiting for transfers between devices  150 us (55%)
  matrix products  38.2 us (14%)
  blocking collectives  29 us (11%)
  other arithmetic  25.1 us (9%)
  between operations  16.5 us (6%)
  starting transfers between devices  8.64 us (3%)
  local copies, waits for them, and re-layouts  4.61 us (2%)
    all_gather x4, waiting for transfers between devices, on_device(): lax.all_gather(piece, 'col', axis=1, tiled=True).reshape(2 * pairs, step)  123 us
    dot_general x16, matrix products, contract(): lax.dot_general(left_side, right_side, (((0,), (0,)), ((), ())), preferre...  38.2 us
    all_gather x1, blocking collectives, on_device(): lax.all_gather(bands, 'col', axis=1, tiled=True).astype(jnp.int32)  29 us
    all_gather x1, waiting for transfers between devices, on_device(): spread = lax.all_gather(both, 'row', axis=2, tiled=True)  24.9 us
    another operation x2, other arithmetic, on_device(): chi_imag = jnp.stack([jnp.concatenate(p, axis=0) for p in imag_parts])  10.8 us
    another operation x2, other arithmetic, on_device(): chi_real = jnp.stack([jnp.concatenate(p, axis=0) for p in real_parts])  9.18 us
    all_to_all x1, starting transfers between devices, on_device(): lax.all_to_all(spread, 'col', split_axis=2, concat_axis=1, tiled=True)  8.44 us
  transfers between devices with their start and end apart: 6, of which 5 were waited for; matrix products, arithmetic and copies ran while one was open for 9% of the time, Pallas kernels for 0%

commit v1 on v0

--- a/solution.py
+++ b/solution.py
@@ -2,6 +2,13 @@
 import jax.numpy as jnp
 from jax import lax
 from jax.sharding import PartitionSpec as P
+
+
+def draw_tails(tile_in, dim_k):
+    answer = list(tile_in.shape[1:])
+    answer[dim_k] *= tile_in.shape[0]
+    b_now = jnp.moveaxis(tile_in, 0, dim_k).reshape(answer)
+    return b_now
 
 
 def lookup(indices, table):
@@ -35,7 +42,27 @@
     bands = jnp.stack([valence_index, conduction_index]).astype(jnp.float32)
     all_bands = lax.all_gather(bands, "col", axis=1, tiled=True).astype(jnp.int32)
     gap = lookup(all_bands[1], conduction_energy) - lookup(all_bands[0], valence_energy)
-    spread = lax.all_gather(both, "row", axis=2, tiled=True)
+    devs = lax.axis_size("row")
+    all_rows = []
+    for k0 in range(devs):
+        all_rows.append((k0, (k0 + 1) % devs))
+    seen = []
+    for tick, j in all_rows:
+        seen.append((j, tick))
+    step_out, u_next = ([], [])
+    for c in range(devs - 1):
+        if c % 2 == 0:
+            u1 = lax.ppermute(step_out[-1] if step_out else both, "row", all_rows)
+            step_out.append(u1)
+        else:
+            item_now = lax.ppermute(u_next[-1] if u_next else both, "row", seen)
+            u_next.append(item_now)
+    after = jnp.stack([*step_out[::-1], both, *u_next], 0)
+    reached = lax.axis_index("row")
+    current_block = len(step_out)
+    d_next = reached - current_block
+    after = after[(jnp.arange(devs) - d_next) % devs]
+    spread = draw_tails(after, 2)
     spread = spread.reshape(2, local_pairs, ncol, -1)
     column = lax.all_to_all(spread, "col", split_axis=2, concat_axis=1, tiled=True)
     width = column.shape[-1]

time: 272 us -> 248 us (0.912)
  waiting for transfers between devices: 150 us -> 116 us
  starting transfers between devices: 8.64 us -> 14.1 us
    all_gather x1 -> x0, waiting for transfers between devices: 24.9 us -> none  [on_device(): spread = lax.all_gather(both, 'row', axis=2, tiled=True)]
    all_gather x4, waiting for transfers between devices: 123 us -> 101 us  [on_device(): lax.all_gather(piece, 'col', axis=1, tiled=True).reshape(2 * pairs, step)]
    ppermute x0 -> x3, waiting for transfers between devices: none -> 13.7 us  [the longest x2 13.7 us: on_device(): u1 = lax.ppermute(step_out[-1] if step_out else both, 'row', all_rows)]
    ppermute x0 -> x3, starting transfers between devices: none -> 4.74 us  [the longest x2 2.54 us: on_device(): u1 = lax.ppermute(step_out[-1] if step_out else both, 'row', all_rows)]
  transfers between devices with their start and end apart: 6 -> 8, of which waited for: 5 -> 5; matrix products, arithmetic and copies ran while one was open for 9% -> 11% of each run, Pallas kernels for 0% -> 0%
where the time goes in v1:
time: 248 us
  waiting for transfers between devices  116 us (47%)
  matrix products  38.8 us (16%)
  blocking collectives  31.2 us (13%)
  other arithmetic  24.6 us (10%)
  between operations  16.5 us (7%)
  starting transfers between devices  14.1 us (6%)
  local copies, waits for them, and re-layouts  6.02 us (2%)
    all_gather x4, waiting for transfers between devices, on_device(): lax.all_gather(piece, 'col', axis=1, tiled=True).reshape(2 * pairs, step)  101 us
    dot_general x16, matrix products, contract(): lax.dot_general(left_side, right_side, (((0,), (0,)), ((), ())), preferre...  38.8 us
    all_gather x1, blocking collectives, on_device(): lax.all_gather(bands, 'col', axis=1, tiled=True).astype(jnp.int32)  31.2 us
    ppermute x2, waiting for transfers between devices, on_device(): u1 = lax.ppermute(step_out[-1] if step_out else both, 'row', all_rows)  13.7 us
    another operation x2, other arithmetic, on_device(): chi_imag = jnp.stack([jnp.concatenate(p, axis=0) for p in imag_parts])  10.8 us
    all_to_all x1, starting transfers between devices, on_device(): lax.all_to_all(spread, 'col', split_axis=2, concat_axis=1, tiled=True)  9.23 us
    another operation x2, other arithmetic, on_device(): chi_real = jnp.stack([jnp.concatenate(p, axis=0) for p in real_parts])  9.18 us
  transfers between devices with their start and end apart: 8, of which 5 were waited for; matrix products, arithmetic and copies ran while one was open for 11% of the time, Pallas kernels for 0%

profile of v1, /device:TPU:1, one launch (start us, length us, event | category | flops | bytes accessed | tf_op | source)
XLA Modules:
  0.0 247.6 jit_solution(5581072987060123237)
XLA Ops:
  7.2 0.0 all-gather.8.cloned.1.call-start
  7.2 1.6 fusion.6
  8.8 0.0 all-gather.8.cloned.1.call-update
  8.8 0.0 all-gather.6.cloned.1.call-start
  8.9 0.7 all-gather.6.cloned.1.call-update
  9.6 0.0 all-gather.10.cloned.1.call-start
  9.6 0.7 all-gather.10.cloned.1.call-update
  10.3 1.0 fusion.13
  11.3 2.5 %collective-permute-start = (bf16[2,16,4096]{2,1,0:T(8,128)(2,1)S(1)}, bf16[2,16,4096]{2,1,0:T(8,128)(2,1)S(1)}, u32[]{:S(2)}, u32[]{:S(2)}) collective-permute-start(bf16[2,16,4096]{2,1,0:T(8,128)(2,1)S(1)} %get-tuple-element.17), channel_id=1, source_target_pairs={{0,32},{32,64},{64,96},{96,0},{1,33},{33,65},{65,97},{97,1},{2,34}... | collective-permute-start | bytes 786440 | tf_op jit(solution)/shard_map/ppermute | solution.py:55
  13.8 2.2 collective-permute-start.2
  16.1 6.0 %collective-permute-done = bf16[2,16,4096]{2,1,0:T(8,128)(2,1)S(1)} collective-permute-done((bf16[2,16,4096]{2,1,0:T(8,128)(2,1)S(1)}, bf16[2,16,4096]{2,1,0:T(8,128)(2,1)S(1)}, u32[]{:S(2)}, u32[]{:S(2)}) %collective-permute-start) | collective-permute-done | bytes 262176 | tf_op jit(solution)/shard_map/ppermute | solution.py:55
  22.0 0.0 collective-permute-done.2
  22.0 7.7 %collective-permute-done.1 = bf16[2,16,4096]{2,1,0:T(8,128)(2,1)S(1)} collective-permute-done((bf16[2,16,4096]{2,1,0:T(8,128)(2,1)S(1)}, bf16[2,16,4096]{2,1,0:T(8,128)(2,1)S(1)}, u32[]{:S(2)}, u32[]{:S(2)}) %collective-permute-start.1) | collective-permute-done | bytes 262176 | tf_op jit(solution)/shard_map/ppermute | solution.py:55
  29.8 0.1 pad_maximum_fusion.2
  29.9 0.6 gather_fusion
  30.5 0.8 copy.25
  31.4 0.8 reshape_reshape.3
  32.2 0.0 copy-start.12
  32.2 0.0 copy-start.15
  32.2 0.0 copy-start.16
  32.2 0.0 copy-start.13
  32.2 0.0 copy-start.14
  32.2 1.5 copy.26
  33.8 9.2 %all-to-all-start = ((bf16[2,16,32,512]{3,1,0,2:T(8,128)(2,1)}), bf16[2,16,32,512]{3,1,0,2:T(8,128)(2,1)S(1)}, u32[]{:S(2)}, u32[]{:S(2)}) async-start(bf16[2,16,32,512]{3,1,0,2:T(8,128)(2,1)} %copy.26), calls=%async_computation | async-start | bytes 2097152 | tf_op jit(solution)/shard_map/all_to_all | solution.py:67
  43.0 0.0 all-gather.12.cloned.1.call-start
  43.1 0.5 all-gather.12.cloned.1.call-update
  43.6 0.6 fusion.20
  46.7 31.2 %all-gather = f32[32,16,2]{1,2,0:T(2,128)S(1)} all-gather(f32[1,16,2]{1,2,0:T(2,128)S(1)} %fusion.10), channel_id=1, replica_groups=mesh['row'=4,'col'=32] {'col'}, dimensions={0}, use_global_device_ids=true | all-gather | bytes 4224 | tf_op jit(solution)/shard_map/all_gather | solution.py:43
  77.9 0.1 copy.23
  78.0 0.1 copy.24
  78.0 0.1 reshape.110
  78.2 0.1 select_reduce_fusion.1
  78.3 0.1 select_reduce_fusion
  78.4 0.3 convert_bitcast_fusion
  78.7 0.2 fusion.18
  78.8 1.4 fusion.5
  80.3 0.0 all-gather.8.cloned.1.call-done
  80.3 4.4 %convolution_convert_fusion.10 = bf16[1024,512]{1,0:T(8,128)(2,1)} fusion(bf16[1024,1024]{1,0:T(8,128)(2,1)} %bitcast.89, bf16[512,512]{1,0:T(8,128)(2,1)S(1)} %get-tuple-element.11, bf16[512,512]{1,0:T(8,128)(2,1)S(1)} %get-tuple-element.18), kind=kOutput, calls=%fused_computation.18 | convolution fusion | flops 1076363264 | bytes 4194304 | tf_op jit(solution)/shard_map/dot_general | solution.py:21
  84.7 24.7 %all-gather.6.cloned.1.call-done = bf16[2,512,1024]{2,1,0:T(8,128)(2,1)} async-done(((bf16[2,16,1024]{2,1,0:T(8,128)(2,1)}), bf16[2,512,1024]{2,1,0:T(8,128)(2,1)}) %all-gather.6.cloned.1.call-update) | async-done | bytes 2097168 | tf_op jit(solution)/shard_map/all_gather | solution.py:84
  109.4 4.0 %convolution_convert_fusion.11 = bf16[1024,512]{1,0:T(8,128)(2,1)} fusion(bf16[1024,1024]{1,0:T(8,128)(2,1)} %bitcast.93, bf16[512,512]{1,0:T(8,128)(2,1)S(1)} %get-tuple-element.11, bf16[512,512]{1,0:T(8,128)(2,1)S(1)} %get-tuple-element.18), kind=kOutput, calls=%fused_computation.19 | convolution fusion | flops 1076363264 | bytes 4194304 | tf_op jit(solution)/shard_map/dot_general | solution.py:21
  113.4 1.3 convolution_convert_fusion.3
  114.7 0.3 copy-done.17
  115.0 2.5 %convolution_convert_fusion.2 = bf16[1024,512]{1,0:T(8,128)(2,1)S(1)} fusion(bf16[1024,1024]{1,0:T(8,128)(2,1)S(1)} %bitcast.90, bf16[512,512]{1,0:T(8,128)(2,1)} %copy-done.8, bf16[512,512]{1,0:T(8,128)(2,1)} %copy-done.5), kind=kOutput, calls=%fused_computation.10 | convolution fusion | flops 1076363264 | bytes 4194304 | tf_op jit(solution)/shard_map/dot_general | solution.py:21
  117.5 37.3 %all-gather.10.cloned.1.call-done = bf16[2,512,1024]{2,1,0:T(8,128)(2,1)} async-done(((bf16[2,16,1024]{2,1,0:T(8,128)(2,1)}), bf16[2,512,1024]{2,1,0:T(8,128)(2,1)}) %all-gather.10.cloned.1.call-update) | async-done | bytes 2097168 | tf_op jit(solution)/shard_map/all_gather | solution.py:84
  154.8 4.2 %convolution_convert_fusion.9 = bf16[1024,512]{1,0:T(8,128)(2,1)} fusion(bf16[1024,1024]{1,0:T(8,128)(2,1)} %bitcast.97, bf16[512,512]{1,0:T(8,128)(2,1)} %copy-done.5, bf16[512,512]{1,0:T(8,128)(2,1)} %copy-done.11), kind=kOutput, calls=%fused_computation.17 | convolution fusion | flops 1076363264 | bytes 4194304 | tf_op jit(solution)/shard_map/dot_general | solution.py:21
  159.0 2.3 convolution_convert_fusion.1
  161.3 38.7 %all-gather.12.cloned.1.call-done = bf16[2,512,1024]{2,1,0:T(8,128)(2,1)} async-done(((bf16[2,16,1024]{2,1,0:T(8,128)(2,1)}), bf16[2,512,1024]{2,1,0:T(8,128)(2,1)}) %all-gather.12.cloned.1.call-update) | async-done | bytes 2097168 | tf_op jit(solution)/shard_map/all_gather | solution.py:84
  200.0 3.3 %convolution_convert_fusion.8 = bf16[1024,512]{1,0:T(8,128)(2,1)S(1)} fusion(bf16[1024,1024]{1,0:T(8,128)(2,1)} %bitcast.101, bf16[512,512]{1,0:T(8,128)(2,1)} %copy-done.5, bf16[512,512]{1,0:T(8,128)(2,1)} %copy-done.11), kind=kOutput, calls=%fused_computation.16 | convolution fusion | flops 1076363264 | bytes 4194304 | tf_op jit(solution)/shard_map/dot_general | solution.py:21
  203.3 2.3 convolution_convert_fusion
  205.6 1.3 convolution_convert_fusion.14
  206.9 0.3 copy-done.22
  207.2 1.3 convolution_convert_fusion.13
  208.5 2.5 %convolution_convert_fusion.6 = bf16[1024,512]{1,0:T(8,128)(2,1)} fusion(bf16[1024,1024]{1,0:T(8,128)(2,1)S(1)} %bitcast.92, bf16[512,512]{1,0:T(8,128)(2,1)S(1)} %copy-done.4, bf16[512,512]{1,0:T(8,128)(2,1)S(1)} %get-tuple-element.10), kind=kOutput, calls=%fused_computation.14 | convolution fusion | flops 1076363264 | bytes 4194304 | tf_op jit(solution)/shard_map/dot_general | solution.py:21
  211.0 2.3 convolution_convert_fusion.5
  213.3 1.3 convolution_convert_fusion.12
  214.6 2.4 convolution_convert_fusion.4
  217.0 2.3 convolution_convert_fusion.7
  219.3 1.3 convolution_convert_fusion.15
  220.6 0.2 copy-done.1
  220.8 0.3 copy-done.2
  221.1 2.8 %maximum_bitcast_fusion = (bf16[1,4096,512]{2,1,0:T(8,128)(2,1)S(1)}, bf16[1,4096,512]{2,1,0:T(8,128)(2,1)}) fusion(bf16[1024,512]{1,0:T(8,128)(2,1)S(1)} %convolution_convert_fusion.12, bf16[1024,512]{1,0:T(8,128)(2,1)S(1)} %convolution_convert_fusion.13, bf16[1024,512]{1,0:T(8,128)(2,1)S(1)} %convolution_convert_fusion.14, ...), kind=kLoop, calls=%fused_computation.3 | loop fusion | flops 33554432 | bytes 16777216 | tf_op jit(solution)/shard_map/stack | solution.py:88
  224.0 6.3 %pad_maximum_fusion = bf16[2,4096,512]{2,1,0:T(8,128)(2,1)} fusion(bf16[1,4096,512]{2,1,0:T(8,128)(2,1)} %get-tuple-element.29, bf16[1,4096,512]{2,1,0:T(8,128)(2,1)S(1)} %get-tuple-element.28), kind=kLoop, calls=%fused_computation.1 | loop fusion | flops 4194304 | bytes 16777216 | tf_op jit(solution)/shard_map/stack | solution.py:88
  230.3 4.4 %maximum_bitcast_fusion.2 = (bf16[1,4096,512]{2,1,0:T(8,128)(2,1)S(1)}, bf16[1,4096,512]{2,1,0:T(8,128)(2,1)}) fusion(bf16[1024,512]{1,0:T(8,128)(2,1)} %convolution_convert_fusion.4, bf16[1024,512]{1,0:T(8,128)(2,1)} %convolution_convert_fusion.5, bf16[1024,512]{1,0:T(8,128)(2,1)} %convolution_convert_fusion.6, ...), kind=kLoop, calls=%fused_computation.5 | loop fusion | flops 33554432 | bytes 16777216 | tf_op jit(solution)/shard_map/stack | solution.py:89
  234.8 6.3 %pad_maximum_fusion.1 = bf16[2,4096,512]{2,1,0:T(8,128)(2,1)} fusion(bf16[1,4096,512]{2,1,0:T(8,128)(2,1)} %get-tuple-element.31, bf16[1,4096,512]{2,1,0:T(8,128)(2,1)S(1)} %get-tuple-element.30), kind=kLoop, calls=%fused_computation.2 | loop fusion | flops 4194304 | bytes 16777216 | tf_op jit(solution)/shard_map/stack | solution.py:89
  (47 shorter events, 0.1 us)
Async XLA Ops:
  7.2 73.1 %all-gather.8.cloned.1.call-start = ((), (), s32[]{:S(2)}) async-start(), calls=%async_computation.2 | async-start | bytes 2162688 | tf_op jit(solution)/shard_map/all_gather | solution.py:84
  8.8 100.6 %all-gather.6.cloned.1.call-start = ((), (), s32[]{:S(2)}) async-start(), calls=%async_computation.1 | async-start | bytes 2162688 | tf_op jit(solution)/shard_map/all_gather | solution.py:84
  9.6 145.2 %all-gather.10.cloned.1.call-start = ((), (), s32[]{:S(2)}) async-start(), calls=%async_computation.3 | async-start | bytes 2162688 | tf_op jit(solution)/shard_map/all_gather | solution.py:84
  11.3 10.7 %collective-permute-start = (bf16[2,16,4096]{2,1,0:T(8,128)(2,1)S(1)}, bf16[2,16,4096]{2,1,0:T(8,128)(2,1)S(1)}, u32[]{:S(2)}, u32[]{:S(2)}) collective-permute-start(bf16[2,16,4096]{2,1,0:T(8,128)(2,1)S(1)} %get-tuple-element.17), channel_id=1, source_target_pairs={{0,32},{32,64},{64,96},{96,0},{1,33},{33,65},{65,97},{97,1},{2,34}... | collective-permute-start | bytes 786440 | tf_op jit(solution)/shard_map/ppermute | solution.py:55
  13.8 8.2 %collective-permute-start.2 = (bf16[2,16,4096]{2,1,0:T(8,128)(2,1)S(1)}, bf16[2,16,4096]{2,1,0:T(8,128)(2,1)S(1)}, u32[]{:S(2)}, u32[]{:S(2)}) collective-permute-start(bf16[2,16,4096]{2,1,0:T(8,128)(2,1)S(1)} %get-tuple-element.17), channel_id=1, source_target_pairs={{32,0},{64,32},{96,64},{0,96},{33,1},{65,33},{97,65},{1,97},{34,2}... | collective-permute-start | bytes 786440 | tf_op jit(solution)/shard_map/ppermute | solution.py:58
  22.0 7.8 %collective-permute-start.1 = (bf16[2,16,4096]{2,1,0:T(8,128)(2,1)S(1)}, bf16[2,16,4096]{2,1,0:T(8,128)(2,1)S(1)}, u32[]{:S(2)}, u32[]{:S(2)}) collective-permute-start(bf16[2,16,4096]{2,1,0:T(8,128)(2,1)S(1)} %collective-permute-done), channel_id=1, source_target_pairs={{0,32},{32,64},{64,96},{96,0},{1,33},{33,65},{65,97},{97,1},{2,34}... | collective-permute-start | bytes 786440 | tf_op jit(solution)/shard_map/ppermute | solution.py:55
  32.2 11.4 %copy-start.12 = (f32[2]{0:T(128)S(1)}, f32[2]{0:T(128)}, u32[]{:S(2)}) copy-start(f32[2]{0:T(128)} %param.13) | copy-start | bytes 28
  32.2 14.5 %copy-start.15 = (s32[16]{0:T(128)S(1)}, s32[16]{0:T(128)}, u32[]{:S(2)}) copy-start(s32[16]{0:T(128)} %param.10) | copy-start | bytes 196
  32.2 14.5 %copy-start.16 = (s32[16]{0:T(128)S(1)}, s32[16]{0:T(128)}, u32[]{:S(2)}) copy-start(s32[16]{0:T(128)} %param.9) | copy-start | bytes 196
  32.2 45.9 %copy-start.13 = (f32[16]{0:T(128)S(1)}, f32[16]{0:T(128)}, u32[]{:S(2)}) copy-start(f32[16]{0:T(128)} %param.11) | copy-start | bytes 196
  32.2 46.0 %copy-start.14 = (f32[32]{0:T(128)S(1)}, f32[32]{0:T(128)}, u32[]{:S(2)}) copy-start(f32[32]{0:T(128)} %param.12) | copy-start | bytes 388
  33.8 44.6 %all-to-all-start = ((bf16[2,16,32,512]{3,1,0,2:T(8,128)(2,1)}), bf16[2,16,32,512]{3,1,0,2:T(8,128)(2,1)S(1)}, u32[]{:S(2)}, u32[]{:S(2)}) async-start(bf16[2,16,32,512]{3,1,0,2:T(8,128)(2,1)} %copy.26), calls=%async_computation | async-start | bytes 2097152 | tf_op jit(solution)/shard_map/all_to_all | solution.py:67
  43.0 157.0 %all-gather.12.cloned.1.call-start = ((), (), s32[]{:S(2)}) async-start(), calls=%async_computation.4 | async-start | bytes 2162688 | tf_op jit(solution)/shard_map/all_gather | solution.py:84
  80.3 29.1 %copy-start.11 = (bf16[512,512]{1,0:T(8,128)(2,1)}, bf16[512,512]{1,0:T(8,128)(2,1)S(1)}, u32[]{:S(2)}) copy-start(bf16[512,512]{1,0:T(8,128)(2,1)S(1)} %get-tuple-element.18) | copy-start | bytes 1572868
  80.3 33.2 %copy-start.5 = (bf16[512,512]{1,0:T(8,128)(2,1)}, bf16[512,512]{1,0:T(8,128)(2,1)S(1)}, u32[]{:S(2)}) copy-start(bf16[512,512]{1,0:T(8,128)(2,1)S(1)} %get-tuple-element.11) | copy-start | bytes 1572868
  80.3 33.2 %copy-start.8 = (bf16[512,512]{1,0:T(8,128)(2,1)}, bf16[512,512]{1,0:T(8,128)(2,1)S(1)}, u32[]{:S(2)}) copy-start(bf16[512,512]{1,0:T(8,128)(2,1)S(1)} %get-tuple-element.19) | copy-start | bytes 1572868
  109.4 4.0 %copy-start.19 = (bf16[2,512,1024]{2,1,0:T(8,128)(2,1)S(1)}, bf16[2,512,1024]{2,1,0:T(8,128)(2,1)}, u32[]{:S(2)}) copy-start(bf16[2,512,1024]{2,1,0:T(8,128)(2,1)} %all-gather.6.cloned.1.call-done) | copy-start | bytes 6291460
  113.4 1.6 copy-start.17
  154.8 4.2 %copy-start.6 = (bf16[512,512]{1,0:T(8,128)(2,1)S(1)}, bf16[512,512]{1,0:T(8,128)(2,1)}, u32[]{:S(2)}) copy-start(bf16[512,512]{1,0:T(8,128)(2,1)} %copy-done.5) | copy-start | bytes 1572868
  154.8 4.2 %copy-start.9 = (bf16[512,512]{1,0:T(8,128)(2,1)S(1)}, bf16[512,512]{1,0:T(8,128)(2,1)}, u32[]{:S(2)}) copy-start(bf16[512,512]{1,0:T(8,128)(2,1)} %copy-done.8) | copy-start | bytes 1572868
  154.8 4.2 %copy-start.21 = (bf16[2,512,1024]{2,1,0:T(8,128)(2,1)S(1)}, bf16[2,512,1024]{2,1,0:T(8,128)(2,1)}, u32[]{:S(2)}) copy-start(bf16[2,512,1024]{2,1,0:T(8,128)(2,1)} %all-gather.10.cloned.1.call-done) | copy-start | bytes 6291460
  200.0 3.3 %copy-start.7 = (bf16[512,512]{1,0:T(8,128)(2,1)S(1)}, bf16[512,512]{1,0:T(8,128)(2,1)}, u32[]{:S(2)}) copy-start(bf16[512,512]{1,0:T(8,128)(2,1)} %copy-done.5) | copy-start | bytes 1572868
  200.0 3.3 %copy-start.10 = (bf16[512,512]{1,0:T(8,128)(2,1)S(1)}, bf16[512,512]{1,0:T(8,128)(2,1)}, u32[]{:S(2)}) copy-start(bf16[512,512]{1,0:T(8,128)(2,1)} %copy-done.8) | copy-start | bytes 1572868
  200.0 3.3 %copy-start.23 = (bf16[2,512,1024]{2,1,0:T(8,128)(2,1)S(1)}, bf16[2,512,1024]{2,1,0:T(8,128)(2,1)}, u32[]{:S(2)}) copy-start(bf16[2,512,1024]{2,1,0:T(8,128)(2,1)} %all-gather.12.cloned.1.call-done) | copy-start | bytes 6291460
  203.3 2.3 copy-start.3
  203.3 2.3 copy-start.18
  205.6 1.6 copy-start.22
  207.2 1.3 copy-start.4
  214.6 2.4 copy-start.20
  219.3 1.3 copy-start
  219.3 1.5 copy-start.1
  219.3 1.9 copy-start.2
Sparse Core Ops, SparseCore 0:
  10.9 55.1 all-gather.7
  68.5 40.8 all-gather.5
  111.8 42.9 all-gather.9
  157.0 42.9 all-gather.11
